TPU v7x, 256 devices: a whole 4x4x8 slice. The times are simulated.
256 devices in a mesh: blk: 32 (over x, y, core), row: 8 (over z).
Axes of the slice: x: 4, y: 4, z: 8, core: 2. Of those that a mesh axis runs over, the one named last changes fastest.
Arguments:
- samples: bfloat16 [1024, 8192], P('blk', 'row'), may hold values from -8 to 8, as said below
- blocks: int32 [64, 4], replicated, may hold values from 0 to 31
- factor: float32 [64, 1024], P(None, 'row'), may hold values from -1.2 to 1.2
Outputs:
- cumulants: float32 [64, 1024, 1024], P('blk', 'row')
- factor_out: float32 [64, 1024], P(None, 'row')
Inputs may be any that keep to these rules, and one draw needn't show every extreme that they name: `samples`: channel values are drawn with mean zero.
All inputs are finite; a program needn't handle non-finite values.
Results may differ from a plain program's by a relative error of at most 0.0014.
Values may be sent and summed in bfloat16 or wider, within the bound.
No kernel may reach another device: no remote copies, remote signals or barrier semaphores. Data moves between devices by JAX's collectives and lax.ppermute only.
A program may use at most 64 MiB of HBM per device.

v0:
```python
import jax
import jax.numpy as jnp
from jax import lax
from jax.sharding import PartitionSpec as P

CHANNELS = 1024
BLOCK = 32
RANK = 64
SAMPLES = 8192
ITERS = 2
step_size = 0.2


def pair_rows(left, right):
    product = left[:, None, :].astype(jnp.float32) * right[None, :, :].astype(jnp.float32)
    return product.reshape(left.shape[0] * right.shape[0], left.shape[1]).astype(jnp.bfloat16)


def contract_last(left, right):
    return lax.dot_general(
        left, right, (((1,), (1,)), ((), ())), preferred_element_type=jnp.float32
    )


def gauss_terms(gram, count, width, row_lo):
    highest = lax.Precision.HIGHEST

    def part(first, second):
        return gram[first * width : (first + 1) * width, second * width : (second + 1) * width]

    cov_ab = lax.dynamic_slice_in_dim(part(0, 1), row_lo, count, 0)
    cov_ac = lax.dynamic_slice_in_dim(part(0, 2), row_lo, count, 0)
    cov_ad = lax.dynamic_slice_in_dim(part(0, 3), row_lo, count, 0)
    cov_cd = part(2, 3)
    cov_bd = part(1, 3)
    cov_bc = part(1, 2)
    first_term = cov_ab.reshape(-1)[:, None] * cov_cd.reshape(-1)[None, :]
    second_term = jnp.einsum("ik,jl->ijkl", cov_ac, cov_bd, precision=highest).reshape(
        count * width, width * width
    )
    third_term = jnp.einsum("il,jk->ijkl", cov_ad, cov_bc, precision=highest).reshape(
        count * width, width * width
    )
    return first_term + second_term + third_term


def add_cols(total, piece, start):
    old = lax.dynamic_slice_in_dim(total, start, piece.shape[1], 1)
    return lax.dynamic_update_slice_in_dim(total, old + piece, start, 1)


def add_grads(total, kslab, full, ids, row_lo, count, width):
    highest = lax.Precision.HIGHEST
    rank = full.shape[0]
    start_a = ids[0] * width + row_lo
    fac_a = lax.dynamic_slice_in_dim(full, start_a, count, 1)
    fac_b = lax.dynamic_slice_in_dim(full, ids[1] * width, width, 1)
    fac_c = lax.dynamic_slice_in_dim(full, ids[2] * width, width, 1)
    fac_d = lax.dynamic_slice_in_dim(full, ids[3] * width, width, 1)
    upair = (fac_a[:, :, None] * fac_b[:, None, :]).reshape(rank, count * width)
    vpair = (fac_c[:, :, None] * fac_d[:, None, :]).reshape(rank, width * width)
    model = lax.dot_general(upair, vpair, (((0,), (0,)), ((), ())), precision=highest)
    resid = kslab - model
    wmat = lax.dot_general(vpair, resid, (((1,), (1,)), ((), ())), precision=highest).reshape(
        rank, count, width
    )
    zmat = jnp.dot(upair, resid, precision=highest).reshape(rank, width, width)
    total = add_cols(total, jnp.sum(wmat * fac_b[:, None, :], axis=2), start_a)
    total = add_cols(total, jnp.sum(wmat * fac_a[:, :, None], axis=1), ids[1] * width)
    total = add_cols(total, jnp.sum(zmat * fac_d[:, None, :], axis=2), ids[2] * width)
    total = add_cols(total, jnp.sum(zmat * fac_c[:, :, None], axis=1), ids[3] * width)
    return total


def gather_factor(columns):
    return lax.all_gather(columns, "row", axis=1, tiled=True)


def per_device(samples, blocks, factor):
    width = BLOCK
    row_count = lax.axis_size("row")
    count = width // row_count
    row_lo = lax.axis_index("row") * count
    per_owner = blocks.shape[0] // lax.axis_size("blk")
    mine = lax.dynamic_slice_in_dim(blocks, lax.axis_index("blk") * per_owner, per_owner, 0)
    needed = mine.reshape(-1)
    pairs = width * width
    piece = lax.all_gather(samples, "blk", axis=0, tiled=True)
    pieces = piece.shape[0] // width
    owned = jnp.arange(pieces, dtype=jnp.int32)
    select = (needed[:, None] == owned[None, :]).astype(jnp.bfloat16)
    shaped = piece.reshape(pieces, width, piece.shape[1])
    taken = jnp.einsum("mb,bcs->mcs", select, shaped, preferred_element_type=jnp.float32)
    local = taken.astype(jnp.bfloat16)
    slabs = []
    whole = lax.all_gather(local, "row", axis=2, tiled=True)
    sample_block = min(SAMPLES, 2048)
    for slot in range(per_owner):
        source_a = whole[4 * slot]
        source_b = whole[4 * slot + 1]
        source_c = whole[4 * slot + 2]
        source_d = whole[4 * slot + 3]

        def accumulate(index, moment):
            low = index * sample_block
            left = lax.dynamic_slice(source_a, (row_lo, low), (count, sample_block))
            right = lax.dynamic_slice_in_dim(source_b, low, sample_block, 1)
            third = lax.dynamic_slice_in_dim(source_c, low, sample_block, 1)
            fourth = lax.dynamic_slice_in_dim(source_d, low, sample_block, 1)
            pmat = pair_rows(left, right)
            qmat = pair_rows(third, fourth)
            return moment + contract_last(pmat, qmat)

        moment = lax.fori_loop(
            0, SAMPLES // sample_block, accumulate, jnp.zeros((count * width, pairs), jnp.float32)
        )
        moment = moment / SAMPLES
        joined = whole[4 * slot : 4 * slot + 4].reshape(4 * width, whole.shape[2])
        gram = contract_last(joined, joined) / SAMPLES
        slabs.append(moment - gauss_terms(gram, count, width, row_lo))
    columns = factor
    full = gather_factor(columns)
    for step in range(ITERS):
        grad = jnp.zeros(full.shape, jnp.float32)
        for slot in range(per_owner):
            grad = add_grads(grad, slabs[slot], full, mine[slot], row_lo, count, width)
        owned_cols = lax.psum_scatter(grad, "row", scatter_dimension=1, tiled=True)
        owned_cols = lax.psum(owned_cols, "blk")
        squares = lax.psum(jnp.sum(owned_cols * owned_cols), "row")
        scale = lax.rsqrt(squares / (RANK * CHANNELS) + 1e-06)
        columns = columns + step_size * scale * owned_cols
        if step + 1 < ITERS:
            full = gather_factor(columns)
    return (jnp.stack(slabs), columns)


def solution(mesh):
    placed = (P("blk", "row"), P(), P(None, "row"))
    return jax.shard_map(
        per_device,
        mesh=mesh,
        in_specs=placed,
        out_specs=(P("blk", "row", None), P(None, "row")),
        check_vma=False,
    )
```

profile of v0, /device:TPU:32, one launch (start us, length us, event | category | flops | bytes accessed | tf_op | source)
XLA Modules:
  0.0 646.9 jit_solution(17991353607669108797)
XLA Ops:
  8.2 53.5 %all-gather.3.cloned.1.call-done = bf16[1024,1024]{1,0:T(8,128)(2,1)} async-done(((bf16[32,1024]{1,0:T(8,128)(2,1)}), bf16[1024,1024]{1,0:T(8,128)(2,1)}) %all-gather.3.cloned.1.call-update) | async-done | bytes 2097168 | tf_op jit(solution)/shard_map/all_gather | solution.py:88
  61.8 4.7 fusion.2
  72.3 26.5 %all_gather.14 = f32[64,1024]{1,0:T(8,128)S(1)} all-gather(f32[64,128]{1,0:T(8,128)S(1)} %copy-done.11), channel_id=1, replica_groups=mesh['blk'=32,'row'=8] {'row'}, dimensions={1}, use_global_device_ids=true | all-gather | bytes 294912 | tf_op jit(solution)/shard_map/all_gather | solution.py:76
  99.6 0.9 broadcast_multiply_fusion.3
  100.4 0.9 broadcast_multiply_fusion.2
  101.3 19.8 %all-gather.5.cloned.1.call-done = bf16[8,32,8192]{2,0,1:T(8,128)(2,1)} async-done(((bf16[8,32,1024]{2,0,1:T(8,128)(2,1)}), bf16[8,32,8192]{2,0,1:T(8,128)(2,1)}) %all-gather.5.cloned.1.call-update) | async-done | bytes 4194320 | tf_op jit(solution)/shard_map/all_gather | solution.py:96
  121.1 21.7 %fusion.10 = (bf16[1,32,8192]{2,0,1:T(2,128)(2,1)S(1)}, bf16[1,32,8192]{2,0,1:T(2,128)(2,1)}, bf16[1,32,8192]{2,0,1:T(2,128)(2,1)}, bf16[1,32,8192]{2,0,1:T(2,12...) fusion(bf16[8,32,8192]{2,0,1:T(8,128)(2,1)} %all-gather.5.clone, ...), kind=kLoop, calls=%fused_computation.112 | loop fusion | bytes 8388608 | tf_op jit(solution)/shard_map/slice | solution.py:102
  142.8 2.0 copy_bitcast_fusion.6
  144.8 1.1 copy_bitcast_fusion.4
  145.9 31.4 %while.32 = (s32[]{:T(128)}, f32[128,1024]{1,0:T(8,128)S(1)}, bf16[32,8192]{1,0:T(8,128)(2,1)}, s32[]{:T(128)}, bf16[32,8192]{1,0:T(8,128)(2,1)S(1)}, /*index=5*...) while((s32[]{:T(128)}, f32[128,1024]{1,0:T(8,128)S(1)}, ...), condition=%wide.region_1.0_spmd.clone, body=%wide.region_0.0_spmd.clone.sunk | while | flops 542056448 | bytes 12533941 | solution.py:114
  146.0 3.0 multiply_convert_fusion.9
  149.1 0.8 dynamic-slice_convert_fusion.15
  150.0 3.8 convolution_add_fusion.4
  153.9 3.0 multiply_convert_fusion.9
  156.9 0.8 dynamic-slice_convert_fusion.15
  157.9 3.8 convolution_add_fusion.4
  161.7 3.0 multiply_convert_fusion.9
  164.8 0.8 dynamic-slice_convert_fusion.15
  165.7 3.8 convolution_add_fusion.4
  169.6 3.0 multiply_convert_fusion.9
  172.6 0.8 dynamic-slice_convert_fusion.15
  173.6 3.8 convolution_add_fusion.4
  177.4 6.7 %fusion.11 = (bf16[4,32,8192]{2,0,1:T(4,128)(2,1)S(1)}, bf16[4,32,8192]{2,0,1:T(4,128)(2,1)}) fusion(bf16[8,32,8192]{2,0,1:T(8,128)(2,1)} %all-gather.5.cloned.1.call-done), kind=kLoop, calls=%fused_computation.113 | loop fusion | bytes 8388608 | tf_op jit(solution)/shard_map/slice | solution.py:118
  184.0 1.2 copy.68
  186.9 1.8 reshape.324
  188.7 2.7 copy.69
  192.6 1.8 reshape.325
  194.5 1.4 add_subtract_fusion.1
  196.5 1.0 copy.75
  197.6 3.6 copy_bitcast_fusion.2
  201.1 2.1 copy_bitcast_fusion
  203.3 35.3 %while.33 = (s32[]{:T(128)}, f32[128,1024]{1,0:T(8,128)S(1)}, bf16[32,8192]{1,0:T(8,128)(2,1)}, s32[]{:T(128)}, bf16[32,8192]{1,0:T(8,128)(2,1)S(1)}, /*index=5*...) while((s32[]{:T(128)}, f32[128,1024]{1,0:T(8,128)S(1)}, ...), condition=%wide.region_3.0_spmd.clone, body=%wide.region_2.0_spmd.clone.sunk | while | flops 542056448 | bytes 12533941 | solution.py:114
  203.3 1.0 dynamic-slice_convert_fusion.19
  204.3 3.0 multiply_convert_fusion.11
  207.3 0.8 dynamic-slice_convert_fusion.18
  208.2 3.8 convolution_add_fusion.5
  212.0 1.0 dynamic-slice_convert_fusion.19
  213.0 3.0 multiply_convert_fusion.11
  217.0 3.8 convolution_add_fusion.5
  220.8 1.0 dynamic-slice_convert_fusion.19
  221.8 3.0 multiply_convert_fusion.11
  224.8 0.8 dynamic-slice_convert_fusion.18
  225.8 3.8 convolution_add_fusion.5
  229.6 1.0 dynamic-slice_convert_fusion.19
  230.6 3.0 multiply_convert_fusion.11
  233.6 0.8 dynamic-slice_convert_fusion.18
  234.6 3.8 convolution_add_fusion.5
  238.9 1.8 reshape.327
  241.0 1.8 reshape.328
  242.9 1.4 add_subtract_fusion
  244.9 1.0 copy.82
  245.9 1.7 multiply_reduce_fusion.6
  250.8 37.1 %reduce-scatter.3.cloned.1.call-done = f32[64,128]{0,1:T(8,128)} async-done(((f32[64,1024]{0,1:T(8,128)}), f32[64,128]{0,1:T(8,128)}) %reduce-scatter.3.cloned.1.call-update) | async-done | bytes 32784 | tf_op jit(solution)/shard_map/reduce_scatter | solution.py:127
  287.9 124.3 %psum.28 = f32[64,128]{0,1:T(8,128)S(1)} all-reduce(f32[64,128]{0,1:T(8,128)} %reduce-scatter.3.cloned.1.call-done), channel_id=1, replica_groups=mesh['blk'=32,'row'=8] {'blk'}, use_global_device_ids=true, to_apply=%region_13.0 | all-reduce | flops 8192 | bytes 65536 | tf_op jit(solution)/shard_map/psum | solution.py:128
  412.9 16.0 %psum.29 = f32[]{:T(128)} all-reduce(f32[]{:T(128)} %multiply_reduce_fusion.13), channel_id=1, replica_groups=mesh['blk'=32,'row'=8] {'row'}, use_global_device_ids=true, to_apply=%region_15.0 | all-reduce | flops 1 | bytes 8 | tf_op jit(solution)/shard_map/psum | solution.py:129
  429.7 24.3 %all_gather.15 = f32[64,1024]{0,1:T(8,128)S(1)} all-gather(f32[64,128]{0,1:T(8,128)S(1)} %multiply_add_fusion.1), channel_id=1, replica_groups=mesh['blk'=32,'row'=8] {'row'}, dimensions={1}, use_global_device_ids=true | all-gather | bytes 294912 | tf_op jit(solution)/shard_map/all_gather | solution.py:76
  454.7 1.0 copy.89
  456.3 1.0 copy.86
  457.3 1.7 multiply_reduce_fusion
  459.7 1.7 multiply_reduce_fusion.2
  463.1 34.0 %reduce-scatter.5.cloned.1.call-done = f32[64,128]{0,1:T(8,128)} async-done(((f32[64,1024]{0,1:T(8,128)}), f32[64,128]{0,1:T(8,128)}) %reduce-scatter.5.cloned.1.call-update) | async-done | bytes 32784 | tf_op jit(solution)/shard_map/reduce_scatter | solution.py:127
  497.1 124.3 %psum.30 = f32[64,128]{0,1:T(8,128)S(1)} all-reduce(f32[64,128]{0,1:T(8,128)} %reduce-scatter.5.cloned.1.call-done), channel_id=1, replica_groups=mesh['blk'=32,'row'=8] {'blk'}, use_global_device_ids=true, to_apply=%region_25.0 | all-reduce | flops 8192 | bytes 65536 | tf_op jit(solution)/shard_map/psum | solution.py:128
  622.0 1.0 pad_maximum_fusion
  623.1 15.9 %psum.31 = f32[]{:T(128)} all-reduce(f32[]{:T(128)} %multiply_reduce_fusion.8), channel_id=1, replica_groups=mesh['blk'=32,'row'=8] {'row'}, use_global_device_ids=true, to_apply=%region_27.0 | all-reduce | flops 1 | bytes 8 | tf_op jit(solution)/shard_map/psum | solution.py:129
  (127 shorter events, 18.1 us)
Async XLA Ops:
  7.2 0.8 copy-start
  7.2 65.1 %copy-start.11 = (f32[64,128]{1,0:T(8,128)S(1)}, f32[64,128]{1,0:T(8,128)}, u32[]{:S(2)}) copy-start(f32[64,128]{1,0:T(8,128)} %param.9) | copy-start | bytes 98308
  7.2 54.6 %all-gather.3.cloned.1.call-start = ((), (), s32[]{:S(2)}) async-start(), calls=%async_computation.2 | async-start | bytes 2162688 | tf_op jit(solution)/shard_map/all_gather | solution.py:88
  7.9 113.2 %all-gather.5.cloned.1.call-start = ((), (), s32[]{:S(2)}) async-start(), calls=%async_computation.3 | async-start | bytes 4718592 | tf_op jit(solution)/shard_map/all_gather | solution.py:96
  66.5 221.4 %reduce-scatter.3.cloned.1.call-start = ((), (), s32[]{:S(2)}) async-start(), calls=%async_computation.4 | async-start | bytes 589824 | tf_op jit(solution)/shard_map/reduce_scatter | solution.py:127
  192.3 2.1 copy-start.12
  194.4 1.5 copy-start.2
  196.5 4.6 copy-start.4
  196.5 4.6 copy-start.6
  197.6 3.6 copy-start.7
  242.8 1.5 copy-start.1
  244.3 3.4 copy-start.3
  244.3 3.4 copy-start.5
  245.9 3.3 copy-start.10
  249.9 0.8 copy-start.9
  250.7 246.3 %reduce-scatter.5.cloned.1.call-start = ((), (), s32[]{:S(2)}) async-start(), calls=%async_computation.5 | async-start | bytes 589824 | tf_op jit(solution)/shard_map/reduce_scatter | solution.py:127
  462.3 0.8 copy-start.8
Sparse Core Ops, SparseCore 0:
  10.6 51.1 all-gather.2
  66.6 54.4 all-gather.4
  250.8 36.9 reduce-scatter.2
  463.2 33.8 reduce-scatter.4
where the time goes:
time: 648 us; the launch traced here: 647 us
  blocking collectives  331 us (51%)
  waiting for transfers between devices  145 us (22%)
  local copies, waits for them, and re-layouts  57.5 us (9%)
  matrix products  47.2 us (7%)
  other arithmetic  44.2 us (7%)
  between operations  20.7 us (3%)
    psum x2, blocking collectives, per_device(): owned_cols = lax.psum(owned_cols, 'blk')  249 us
    reduce_scatter x2, waiting for transfers between devices, per_device(): owned_cols = lax.psum_scatter(grad, 'row', scatter_dimension=1, tiled=True)  71.1 us
    all_gather x1, waiting for transfers between devices, per_device(): piece = lax.all_gather(samples, 'blk', axis=0, tiled=True)  53.5 us
    all_gather x2, blocking collectives, gather_factor(): return lax.all_gather(columns, 'row', axis=1, tiled=True)  50.7 us
    psum x2, blocking collectives, per_device(): squares = lax.psum(jnp.sum(owned_cols * owned_cols), 'row')  32 us
    dot_general x10, matrix products, contract_last(): lax.dot_general(left, right, (((1,), (1,)), ((), ())), preferred_element_...  31.6 us
    convert_element_type x16, other arithmetic, pair_rows(): product.reshape(left.shape[0] * right.shape[0], left.shape[1])  24.8 us
    slice x1, local copies, waits for them, and re-layouts, per_device(): source_d = whole[4 * slot + 3]  21.7 us
  transfers between devices with their start and end apart: 4, of which 4 were waited for; matrix products, arithmetic and copies ran while one was open for 1% of the time, Pallas kernels for 0%

commit v1 on v0

--- a/solution.py
+++ b/solution.py
@@ -85,7 +85,9 @@
     mine = lax.dynamic_slice_in_dim(blocks, lax.axis_index("blk") * per_owner, per_owner, 0)
     needed = mine.reshape(-1)
     pairs = width * width
-    piece = lax.all_gather(samples, "blk", axis=0, tiled=True)
+    piece = jnp.concatenate(
+        lax.all_to_all(jnp.stack([samples] * lax.axis_size("blk")), "blk", 0, 0), axis=0
+    )
     pieces = piece.shape[0] // width
     owned = jnp.arange(pieces, dtype=jnp.int32)
     select = (needed[:, None] == owned[None, :]).astype(jnp.bfloat16)

time: 648 us -> 630 us (0.972)
  waiting for transfers between devices: 145 us -> 116 us
  starting transfers between devices: 0.16 us -> 7.44 us
    all_gather x1 -> x0, waiting for transfers between devices: 53.5 us -> none  [per_device(): piece = lax.all_gather(samples, 'blk', axis=0, tiled=True)]
    all_to_all x0 -> x1, waiting for transfers between devices: none -> 28.6 us  [per_device(): lax.all_to_all(jnp.stack([samples] * lax.axis_size('blk')), 'blk', 0, 0)]
    all_to_all x0 -> x1, starting transfers between devices: none -> 7.32 us  [per_device(): lax.all_to_all(jnp.stack([samples] * lax.axis_size('blk')), 'blk', 0, 0)]
where the time goes in v1:
time: 630 us; the launch traced here: 628 us
  blocking collectives  334 us (53%)
  waiting for transfers between devices  116 us (18%)
  local copies, waits for them, and re-layouts  60 us (10%)
  matrix products  45.6 us (7%)
  other arithmetic  44.2 us (7%)
  between operations  20.7 us (3%)
  starting transfers between devices  7.44 us (1%)
    psum x2, blocking collectives, per_device(): owned_cols = lax.psum(owned_cols, 'blk')  249 us
    reduce_scatter x2, waiting for transfers between devices, per_device(): owned_cols = lax.psum_scatter(grad, 'row', scatter_dimension=1, tiled=True)  70.8 us
    all_gather x2, blocking collectives, gather_factor(): return lax.all_gather(columns, 'row', axis=1, tiled=True)  52.9 us
    psum x2, blocking collectives, per_device(): squares = lax.psum(jnp.sum(owned_cols * owned_cols), 'row')  32 us
    dot_general x10, matrix products, contract_last(): lax.dot_general(left, right, (((1,), (1,)), ((), ())), preferred_element_...  31.6 us
    all_to_all x1, waiting for transfers between devices, per_device(): lax.all_to_all(jnp.stack([samples] * lax.axis_size('blk')), 'blk', 0, 0)  28.6 us
    convert_element_type x16, other arithmetic, pair_rows(): product.reshape(left.shape[0] * right.shape[0], left.shape[1])  24.8 us
    slice x1, local copies, waits for them, and re-layouts, per_device(): source_d = whole[4 * slot + 3]  21.7 us
  transfers between devices with their start and end apart: 4, of which 4 were waited for; matrix products, arithmetic and copies ran while one was open for 1% of the time, Pallas kernels for 0%

profile of v1, /device:TPU:32, one launch (start us, length us, event | category | flops | bytes accessed | tf_op | source)
XLA Modules:
  0.0 628.5 jit_solution(16190913677927137950)
XLA Ops:
  7.2 2.5 stack.8
  9.6 7.3 %all-to-all-start = ((bf16[32,32,1024]{2,1,0:T(8,128)(2,1)}), bf16[32,32,1024]{2,1,0:T(8,128)(2,1)S(1)}, u32[]{:S(2)}, u32[]{:S(2)}) async-start(bf16[32,32,1024]{2,1,0:T(8,128)(2,1)} %stack.8), calls=%async_computation | async-start | bytes 4194304 | tf_op jit(solution)/shard_map/all_to_all | solution.py:89
  17.3 28.6 %all-to-all-done = bf16[32,32,1024]{2,1,0:T(8,128)(2,1)S(1)} async-done(((bf16[32,32,1024]{2,1,0:T(8,128)(2,1)}), bf16[32,32,1024]{2,1,0:T(8,128)(2,1)S(1)}, u32[]{:S(2)}, u32[]{:S(2)}) %all-to-all-start) | async-done | bytes 2097184 | tf_op jit(solution)/shard_map/all_to_all | solution.py:89
  45.9 3.1 fusion.2
  54.8 28.6 %all_gather.10 = f32[64,1024]{1,0:T(8,128)S(1)} all-gather(f32[64,128]{1,0:T(8,128)S(1)} %copy-done.11), channel_id=1, replica_groups=mesh['blk'=32,'row'=8] {'row'}, dimensions={1}, use_global_device_ids=true | all-gather | bytes 294912 | tf_op jit(solution)/shard_map/all_gather | solution.py:76
  84.3 0.9 broadcast_multiply_fusion.3
  85.1 0.9 broadcast_multiply_fusion.2
  86.0 16.9 %all-gather.2.cloned.1.call-done = bf16[8,32,8192]{2,0,1:T(8,128)(2,1)} async-done(((bf16[8,32,1024]{2,0,1:T(8,128)(2,1)}), bf16[8,32,8192]{2,0,1:T(8,128)(2,1)}) %all-gather.2.cloned.1.call-update) | async-done | bytes 4194320 | tf_op jit(solution)/shard_map/all_gather | solution.py:98
  102.9 21.7 %fusion.10 = (bf16[1,32,8192]{2,0,1:T(2,128)(2,1)S(1)}, bf16[1,32,8192]{2,0,1:T(2,128)(2,1)}, bf16[1,32,8192]{2,0,1:T(2,128)(2,1)}, bf16[1,32,8192]{2,0,1:T(2,12...) fusion(bf16[8,32,8192]{2,0,1:T(8,128)(2,1)} %all-gather.2.clone, ...), kind=kLoop, calls=%fused_computation.112 | loop fusion | bytes 8388608 | tf_op jit(solution)/shard_map/slice | solution.py:104
  124.7 2.0 copy_bitcast_fusion.6
  126.6 1.1 copy_bitcast_fusion.4
  127.8 31.4 %while.32 = (s32[]{:T(128)}, f32[128,1024]{1,0:T(8,128)S(1)}, bf16[32,8192]{1,0:T(8,128)(2,1)}, s32[]{:T(128)}, bf16[32,8192]{1,0:T(8,128)(2,1)S(1)}, /*index=5*...) while((s32[]{:T(128)}, f32[128,1024]{1,0:T(8,128)S(1)}, ...), condition=%wide.region_1.0_spmd.clone, body=%wide.region_0.0_spmd.clone.sunk | while | flops 542056448 | bytes 12533941 | solution.py:116
  127.8 3.0 multiply_convert_fusion.9
  130.9 0.8 dynamic-slice_convert_fusion.15
  131.8 3.8 convolution_add_fusion.4
  135.7 3.0 multiply_convert_fusion.9
  139.7 3.8 convolution_add_fusion.4
  143.5 3.0 multiply_convert_fusion.9
  146.6 0.8 dynamic-slice_convert_fusion.15
  147.5 3.8 convolution_add_fusion.4
  151.4 3.0 multiply_convert_fusion.9
  154.4 0.8 dynamic-slice_convert_fusion.15
  155.4 3.8 convolution_add_fusion.4
  159.2 6.7 %fusion.11 = (bf16[4,32,8192]{2,0,1:T(4,128)(2,1)S(1)}, bf16[4,32,8192]{2,0,1:T(4,128)(2,1)}) fusion(bf16[8,32,8192]{2,0,1:T(8,128)(2,1)} %all-gather.2.cloned.1.call-done), kind=kLoop, calls=%fused_computation.113 | loop fusion | bytes 8388608 | tf_op jit(solution)/shard_map/slice | solution.py:120
  165.9 1.2 copy.67
  168.7 1.8 reshape.322
  170.5 2.7 copy.68
  174.4 1.8 reshape.323
  176.4 1.4 add_subtract_fusion.1
  178.3 1.0 copy.74
  179.4 3.6 copy_bitcast_fusion.2
  183.0 2.1 copy_bitcast_fusion
  185.1 35.3 %while.33 = (s32[]{:T(128)}, f32[128,1024]{1,0:T(8,128)S(1)}, bf16[32,8192]{1,0:T(8,128)(2,1)}, s32[]{:T(128)}, bf16[32,8192]{1,0:T(8,128)(2,1)S(1)}, /*index=5*...) while((s32[]{:T(128)}, f32[128,1024]{1,0:T(8,128)S(1)}, ...), condition=%wide.region_3.0_spmd.clone, body=%wide.region_2.0_spmd.clone.sunk | while | flops 542056448 | bytes 12533941 | solution.py:116
  185.1 1.0 dynamic-slice_convert_fusion.19
  186.1 3.0 multiply_convert_fusion.11
  189.1 0.8 dynamic-slice_convert_fusion.18
  190.0 3.8 convolution_add_fusion.5
  193.9 1.0 dynamic-slice_convert_fusion.19
  194.9 3.0 multiply_convert_fusion.11
  197.9 0.8 dynamic-slice_convert_fusion.18
  198.8 3.8 convolution_add_fusion.5
  202.6 1.0 dynamic-slice_convert_fusion.19
  203.6 3.0 multiply_convert_fusion.11
  207.6 3.8 convolution_add_fusion.5
  211.4 1.0 dynamic-slice_convert_fusion.19
  212.4 3.0 multiply_convert_fusion.11
  216.4 3.8 convolution_add_fusion.5
  220.7 1.8 reshape.325
  222.8 1.8 reshape.326
  224.7 1.4 add_subtract_fusion
  226.7 1.0 copy.81
  227.7 1.7 multiply_reduce_fusion.6
  232.6 36.8 %reduce-scatter.3.cloned.1.call-done = f32[64,128]{0,1:T(8,128)} async-done(((f32[64,1024]{0,1:T(8,128)}), f32[64,128]{0,1:T(8,128)}) %reduce-scatter.3.cloned.1.call-update) | async-done | bytes 32784 | tf_op jit(solution)/shard_map/reduce_scatter | solution.py:129
  269.4 124.3 %psum.28 = f32[64,128]{0,1:T(8,128)S(1)} all-reduce(f32[64,128]{0,1:T(8,128)} %reduce-scatter.3.cloned.1.call-done), channel_id=1, replica_groups=mesh['blk'=32,'row'=8] {'blk'}, use_global_device_ids=true, to_apply=%region_13.0 | all-reduce | flops 8192 | bytes 65536 | tf_op jit(solution)/shard_map/psum | solution.py:130
  394.4 16.0 %psum.29 = f32[]{:T(128)} all-reduce(f32[]{:T(128)} %multiply_reduce_fusion.13), channel_id=1, replica_groups=mesh['blk'=32,'row'=8] {'row'}, use_global_device_ids=true, to_apply=%region_15.0 | all-reduce | flops 1 | bytes 8 | tf_op jit(solution)/shard_map/psum | solution.py:131
  411.2 24.3 %all_gather.11 = f32[64,1024]{0,1:T(8,128)S(1)} all-gather(f32[64,128]{0,1:T(8,128)S(1)} %multiply_add_fusion.1), channel_id=1, replica_groups=mesh['blk'=32,'row'=8] {'row'}, dimensions={1}, use_global_device_ids=true | all-gather | bytes 294912 | tf_op jit(solution)/shard_map/all_gather | solution.py:76
  436.2 1.0 copy.88
  437.8 1.0 copy.85
  438.8 1.7 multiply_reduce_fusion
  441.2 1.7 multiply_reduce_fusion.2
  444.6 34.0 %reduce-scatter.5.cloned.1.call-done = f32[64,128]{0,1:T(8,128)} async-done(((f32[64,1024]{0,1:T(8,128)}), f32[64,128]{0,1:T(8,128)}) %reduce-scatter.5.cloned.1.call-update) | async-done | bytes 32784 | tf_op jit(solution)/shard_map/reduce_scatter | solution.py:129
  478.6 124.3 %psum.30 = f32[64,128]{0,1:T(8,128)S(1)} all-reduce(f32[64,128]{0,1:T(8,128)} %reduce-scatter.5.cloned.1.call-done), channel_id=1, replica_groups=mesh['blk'=32,'row'=8] {'blk'}, use_global_device_ids=true, to_apply=%region_25.0 | all-reduce | flops 8192 | bytes 65536 | tf_op jit(solution)/shard_map/psum | solution.py:130
  603.5 1.0 pad_maximum_fusion
  604.6 15.9 %psum.31 = f32[]{:T(128)} all-reduce(f32[]{:T(128)} %multiply_reduce_fusion.8), channel_id=1, replica_groups=mesh['blk'=32,'row'=8] {'row'}, use_global_device_ids=true, to_apply=%region_27.0 | all-reduce | flops 1 | bytes 8 | tf_op jit(solution)/shard_map/psum | solution.py:131
  (127 shorter events, 19.0 us)
Async XLA Ops:
  7.2 9.9 %copy-start = (s32[64,4]{0,1:T(4,128)S(1)}, s32[64,4]{0,1:T(4,128)}, u32[]{:S(2)}) copy-start(s32[64,4]{0,1:T(4,128)} %param.8) | copy-start | bytes 3076
  9.6 36.3 %all-to-all-start = ((bf16[32,32,1024]{2,1,0:T(8,128)(2,1)}), bf16[32,32,1024]{2,1,0:T(8,128)(2,1)S(1)}, u32[]{:S(2)}, u32[]{:S(2)}) async-start(bf16[32,32,1024]{2,1,0:T(8,128)(2,1)} %stack.8), calls=%async_computation | async-start | bytes 4194304 | tf_op jit(solution)/shard_map/all_to_all | solution.py:89
  17.0 37.8 %copy-start.11 = (f32[64,128]{1,0:T(8,128)S(1)}, f32[64,128]{1,0:T(8,128)}, u32[]{:S(2)}) copy-start(f32[64,128]{1,0:T(8,128)} %param.9) | copy-start | bytes 98308
  17.0 86.0 %all-gather.2.cloned.1.call-start = ((), (), s32[]{:S(2)}) async-start(), calls=%async_computation.3 | async-start | bytes 4718592 | tf_op jit(solution)/shard_map/all_gather | solution.py:98
  49.0 220.4 %reduce-scatter.3.cloned.1.call-start = ((), (), s32[]{:S(2)}) async-start(), calls=%async_computation.4 | async-start | bytes 589824 | tf_op jit(solution)/shard_map/reduce_scatter | solution.py:129
  174.1 2.1 copy-start.12
  176.2 1.5 copy-start.2
  178.3 4.6 copy-start.4
  178.3 4.6 copy-start.6
  179.4 3.6 copy-start.7
  224.6 1.5 copy-start.1
  226.1 3.4 copy-start.3
  226.1 3.4 copy-start.5
  227.7 3.3 copy-start.10
  231.7 0.8 copy-start.9
  232.5 246.1 %reduce-scatter.5.cloned.1.call-start = ((), (), s32[]{:S(2)}) async-start(), calls=%async_computation.5 | async-start | bytes 589824 | tf_op jit(solution)/shard_map/reduce_scatter | solution.py:129
  443.8 0.8 copy-start.8
Sparse Core Ops, SparseCore 0:
  49.1 53.7 all-gather.1
  232.7 36.6 reduce-scatter.2
  444.7 33.8 reduce-scatter.4
